TPU v7x, 512 devices: a whole 4x8x8 slice. The times are simulated.
512 devices in a mesh: row: 8 (over x, y_lo), col: 8 (over y_hi, core), smp: 8 (over z).
Axes of the slice: x: 4, y: 8 (y_hi: 4, y_lo: 2; y = y_hi * 2 + y_lo), z: 8, core: 2. Of those that a mesh axis runs over, the one named last changes fastest.
Arguments:
- single: bfloat16 [1024, 768], P('row'), may hold values from -0.59765625 to 0.59765625
- pair_features: bfloat16 [1024, 1024, 128], P('row', ('col', 'smp')), may hold values from -6 to 6
- coords: float32 [3, 8192], replicated, may hold values from -6 to 6
- token_centre_atom: int32 [1024], P('row'), may hold values from 0 to 8191
- chain_label: int32 [1024], P('row'), may hold values from 0 to 7, never falling along the last dimension, each value on 1 to 256 neighbouring positions
- padding_key_mask: int32 [1024], P('row'), may hold values 0 or 1
- angles: float32 [8, 3], P('smp'), may hold values from -3.140625 to 3.140625
- sample_noise_level: float32 [8], P('smp'), may hold values from 0.05 to 10
- centre_noise: float32 [8, 3, 1024], P('smp', None, 'row'), may hold values from -6 to 6
- embedding_weight: float32 [4, 768], replicated, may hold values from -1.5 to 1.5
- pair_bias_weight: bfloat16 [128, 4, 16], replicated, may hold values from -1 to 1
- same_chain_offset: float32 [4, 16], replicated, may hold values from -300 to 300
- query_key_value_gate_weight: bfloat16 [4, 4, 768, 768], P(None, None, 'col'), may hold values from -0.21875 to 0.21875
- attention_output_weight: bfloat16 [4, 768, 768], P(None, 'col'), may hold values from -1.25 to 1.25
- position_update_weight: bfloat16 [3, 768], replicated, may hold values from -0.21875 to 0.21875
Outputs:
- tokens_out: bfloat16 [8, 1024, 768], P('smp', 'row')
- denoised: float32 [8, 3, 1024], P('smp', None, 'row')
All inputs are finite; a program needn't handle non-finite values. No bound on the sum of `padding_key_mask` on one device may be relied on, other than what follows from the above.
Results may differ from a plain program's by a relative error of at most 0.024.
Values may be sent and summed in bfloat16 or wider, within the bound.
No kernel may reach another device: no remote copies, remote signals or barrier semaphores. Data moves between devices by JAX's collectives and lax.ppermute only.
A program may use at most 64 MiB of HBM per device.

v0:
```python
import jax
import jax.numpy as jnp
from jax import lax
from jax.sharding import PartitionSpec as P

EPSILON = 1e-05
MASKED = -1000000000.0
LOWEST = -1e30


def layer_norm(inputs):
    average = jnp.mean(inputs, axis=-1, keepdims=True)
    centred = inputs - average
    spread = jnp.mean(centred * centred, axis=-1, keepdims=True)
    return centred * lax.rsqrt(spread + EPSILON)


def rotation_rows(angles):
    cos_a = jnp.cos(angles[:, 0])
    sin_a = jnp.sin(angles[:, 0])
    cos_b = jnp.cos(angles[:, 1])
    sin_b = jnp.sin(angles[:, 1])
    cos_c = jnp.cos(angles[:, 2])
    sin_c = jnp.sin(angles[:, 2])
    first = jnp.stack(
        [
            cos_a * cos_b,
            cos_a * sin_b * sin_c - sin_a * cos_c,
            cos_a * sin_b * cos_c + sin_a * sin_c,
        ],
        axis=-1,
    )
    second = jnp.stack(
        [
            sin_a * cos_b,
            sin_a * sin_b * sin_c + cos_a * cos_c,
            sin_a * sin_b * cos_c - cos_a * sin_c,
        ],
        axis=-1,
    )
    third = jnp.stack([-sin_b, cos_b * sin_c, cos_b * cos_c], axis=-1)
    return jnp.stack([first, second, third], axis=1)


def noisy_centres(coords, token_centre_atom, angles, sample_noise_level, centre_noise):
    centre = jnp.take(coords, token_centre_atom, axis=1)
    rotation = rotation_rows(angles)
    turned = rotation[:, :, 0, None] * centre[0][None, None, :]
    turned = turned + rotation[:, :, 1, None] * centre[1][None, None, :]
    turned = turned + rotation[:, :, 2, None] * centre[2][None, None, :]
    return turned + sample_noise_level[:, None, None] * centre_noise


def embed_tokens(single, noisy, sample_noise_level, embedding_weight):
    scaled = noisy / jnp.sqrt(sample_noise_level * sample_noise_level + 1.0)[:, None, None]
    log_level = 0.25 * jnp.log(sample_noise_level)
    hidden_activity = single.astype(jnp.float32)[None] + scaled[:, 0, :, None] * embedding_weight[0]
    hidden_activity = hidden_activity + scaled[:, 1, :, None] * embedding_weight[1]
    hidden_activity = hidden_activity + scaled[:, 2, :, None] * embedding_weight[2]
    hidden_activity = hidden_activity + log_level[:, None, None] * embedding_weight[3]
    return hidden_activity.astype(jnp.bfloat16)


def relay_bias(local_bias):
    blocks, total_heads, row_count, keys_dev = local_bias.shape
    col_count = lax.axis_size("col")
    copies = lax.axis_size("smp")
    group_members = total_heads // col_count
    spread = jnp.broadcast_to(
        local_bias.reshape(blocks, col_count, 1, group_members, row_count, 1, keys_dev),
        (blocks, col_count, copies, group_members, row_count, 1, keys_dev),
    )
    spread = spread.reshape(blocks, col_count * copies * group_members, row_count, 1, keys_dev)
    relayed = lax.all_to_all(spread, ("col", "smp"), split_axis=1, concat_axis=3, tiled=True)
    return relayed.reshape(blocks, group_members, row_count, -1)


def build_absorber(
    query_vectors,
    per_block_bias,
    chain_offset,
    query_chain_labels,
    gathered_chain_ids,
    gathered_key_mask,
    input_scaling,
):
    samples, row_count, group_members, head_size = query_vectors.shape

    def absorb(running, kv_piece, key_start):
        key_count = kv_piece.shape[0]
        key_rows = kv_piece[:, :, 0].reshape(key_count, samples, group_members, head_size)
        value_rows = kv_piece[:, :, 1].reshape(key_count, samples, group_members, head_size)
        attention_logits = (
            jnp.einsum(
                "sqhd,kshd->shqk", query_vectors, key_rows, preferred_element_type=jnp.float32
            )
            * input_scaling
        )
        bias_section = per_block_bias.astype(jnp.float32)
        chain_match = (query_chain_labels[:, None] == gathered_chain_ids[None, :]).astype(
            jnp.float32
        )
        attention_logits = (
            attention_logits
            + bias_section[None]
            + chain_offset[None, :, None, None] * chain_match[None, None]
        )
        attention_logits = jnp.where(
            gathered_key_mask[None, None, None, :] > 0, attention_logits, MASKED
        )
        old_max, old_sum, old_acc = running
        new_max = jnp.maximum(old_max, jnp.max(attention_logits, axis=-1))
        unscaled = jnp.exp(attention_logits - new_max[..., None])
        new_sum = jnp.sum(unscaled, axis=-1)
        new_acc = jnp.einsum(
            "shqk,kshd->shqd",
            unscaled.astype(jnp.bfloat16),
            value_rows,
            preferred_element_type=jnp.float32,
        )
        return (new_max, new_sum, new_acc)

    return absorb


def body(
    single,
    pair_features,
    coords,
    token_centre_atom,
    chain_label,
    padding_key_mask,
    angles,
    sample_noise_level,
    centre_noise,
    embedding_weight,
    pair_bias_weight,
    same_chain_offset,
    query_key_value_gate_weight,
    attention_output_weight,
    position_update_weight,
):
    noisy = noisy_centres(coords, token_centre_atom, angles, sample_noise_level, centre_noise)
    hidden_activity = embed_tokens(single, noisy, sample_noise_level, embedding_weight)
    pair_normed = layer_norm(pair_features.astype(jnp.float32)).astype(jnp.bfloat16)
    local_bias = jnp.einsum(
        "ikc,cbh->bhik", pair_normed, pair_bias_weight, preferred_element_type=jnp.float32
    ).astype(jnp.bfloat16)
    gathered_pair_bias = relay_bias(local_bias)
    gathered_chain_ids, gathered_key_mask = (
        lax.all_gather(chain_label, "row", axis=0, tiled=True),
        lax.all_gather(padding_key_mask, "row", axis=0, tiled=True),
    )
    samples, row_count, model_width = hidden_activity.shape
    group_members = gathered_pair_bias.shape[1]
    head_size = query_key_value_gate_weight.shape[2] // group_members
    group_offset = lax.axis_index("col") * group_members
    input_scaling = head_size ** (-0.5)
    for block_index in range(query_key_value_gate_weight.shape[0]):
        normed = layer_norm(hidden_activity.astype(jnp.float32)).astype(jnp.bfloat16)
        front = jnp.einsum(
            "snd,fed->fsne",
            normed,
            query_key_value_gate_weight[block_index, 0:2],
            preferred_element_type=jnp.float32,
        )
        key_value = jnp.einsum(
            "snd,fed->nsfe",
            normed,
            query_key_value_gate_weight[block_index, 2:4],
            preferred_element_type=jnp.float32,
        ).astype(jnp.bfloat16)
        query_vectors = (
            front[0].astype(jnp.bfloat16).reshape(samples, row_count, group_members, head_size)
        )
        chain_offset = lax.dynamic_slice_in_dim(
            same_chain_offset[block_index], group_offset, group_members, 0
        )
        absorb = build_absorber(
            query_vectors,
            gathered_pair_bias[block_index],
            chain_offset,
            chain_label,
            gathered_chain_ids,
            gathered_key_mask,
            input_scaling,
        )
        start_state = (
            jnp.full((samples, group_members, row_count), LOWEST, jnp.float32),
            jnp.zeros((samples, group_members, row_count), jnp.float32),
            jnp.zeros((samples, group_members, row_count, head_size), jnp.float32),
        )
        final_max, final_sum, final_acc = absorb(
            start_state, lax.all_gather(key_value, "row", axis=0, tiled=True), jnp.int32(0)
        )
        attended = final_acc / final_sum[..., None]
        attended = jnp.transpose(attended, (0, 2, 1, 3)).reshape(
            samples, row_count, group_members * head_size
        )
        gated_output = (jax.nn.sigmoid(front[1]) * attended).astype(jnp.bfloat16)
        partial_out = jnp.einsum(
            "kxp,pj->kxj",
            gated_output,
            attention_output_weight[block_index],
            preferred_element_type=jnp.float32,
        )
        summed = lax.psum(partial_out.astype(jnp.bfloat16), "col").astype(jnp.float32)
        hidden_activity = (hidden_activity.astype(jnp.float32) + summed).astype(jnp.bfloat16)
    final_normed = layer_norm(hidden_activity.astype(jnp.float32)).astype(jnp.bfloat16)
    update = jnp.einsum(
        "snd,cd->scn", final_normed, position_update_weight, preferred_element_type=jnp.float32
    )
    spread_sq = 1.0 + sample_noise_level * sample_noise_level
    denoised = (
        noisy / spread_sq[:, None, None]
        + (sample_noise_level / jnp.sqrt(spread_sq))[:, None, None] * update
    )
    return (hidden_activity, denoised)


def solution(mesh):
    return jax.shard_map(
        body,
        mesh=mesh,
        in_specs=(
            P("row", None),
            P("row", ("col", "smp"), None),
            P(),
            P("row"),
            P("row"),
            P("row"),
            P("smp", None),
            P("smp"),
            P("smp", None, "row"),
            P(),
            P(),
            P(),
            P(None, None, "col", None),
            P(None, "col", None),
            P(),
        ),
        out_specs=(P("smp", "row", None), P("smp", None, "row")),
        check_vma=False,
    )
```

profile of v0, /device:TPU:17, one launch (start us, length us, event | category | flops | bytes accessed | tf_op | source)
XLA Modules:
  0.0 548.1 jit_solution(17188569693350493762)
XLA Ops:
  7.2 1.4 convert_reduce_fusion
  8.6 1.7 fusion.36
  10.3 1.6 fusion.50
  12.4 1.9 broadcast_in_dim.47
  14.3 16.9 %all-to-all-start = ((bf16[4,128,128,1,16]{2,4,3,0,1:T(8,128)(2,1)}), bf16[4,128,128,1,16]{2,4,3,0,1:T(8,128)(2,1)S(1)}, u32[]{:S(2)}, u32[]{:S(2)}) async-start(bf16[4,128,128,1,16]{2,4,3,0,1:T(8,128)(2,1)} %bitcast.262), calls=%async_computation | async-start | bytes 4194304 | tf_op jit(solution)/shard_map/all_to_all | solution.py:74
  31.3 0.6 fusion.149
  36.9 2.6 copy.35
  39.5 2.8 gather_fusion
  43.7 1.3 convolution_bitcast_fusion.3
  45.0 41.1 %all-gather.1 = s32[8,1,128]{2,1,0:T(1,128)S(1)} all-gather(s32[1,1,128]{2,1,0:T(1,128)S(1)} %bitcast.290), channel_id=1, replica_groups=mesh['row'=8,'col'=8,'smp'=8] {'row'}, dimensions={0}, use_global_device_ids=true | all-gather | bytes 4608 | tf_op jit(solution)/shard_map/all_gather | solution.py:151
  86.1 11.5 %all-gather = s32[8,1,128]{2,1,0:T(1,128)S(1)} all-gather(s32[1,1,128]{2,1,0:T(1,128)S(1)} %bitcast.291), channel_id=1, replica_groups=mesh['row'=8,'col'=8,'smp'=8] {'row'}, dimensions={0}, use_global_device_ids=true | all-gather | bytes 4608 | tf_op jit(solution)/shard_map/all_gather | solution.py:152
  97.7 1.3 fusion.22
  99.0 21.4 %all_gather.19 = bf16[1024,1,2,96]{0,3,2,1:T(8,128)(2,1)S(1)} all-gather(bf16[128,1,2,96]{0,3,2,1:T(8,128)(2,1)S(1)} %fusion.22), channel_id=1, replica_groups=mesh['row'=8,'col'=8,'smp'=8] {'row'}, dimensions={0}, use_global_device_ids=true | all-gather | bytes 442368 | tf_op jit(solution)/shard_map/all_gather | solution.py:194
  121.0 1.9 slice_convert_fusion
  122.9 1.3 copy.42
  124.2 1.7 fusion.150
  126.6 1.8 fusion.14
  128.5 1.3 copy.43
  129.8 1.4 copy.44
  131.2 85.6 %all-reduce.5.cloned.1.call-done = bf16[1,128,768]{2,1,0:T(8,128)(2,1)} async-done(((bf16[1,128,768]{2,1,0:T(8,128)(2,1)}), bf16[1,128,768]{2,1,0:T(8,128)(2,1)}) %all-reduce.5.cloned.1.call-update) | async-done | bytes 196624 | tf_op jit(solution)/shard_map/psum | solution.py:207
  216.9 1.1 convert_reduce_fusion.3
  218.1 1.3 fusion.23
  219.4 1.3 convolution_bitcast_fusion.2
  220.7 21.4 %all_gather.21 = bf16[1024,1,2,96]{0,3,2,1:T(8,128)(2,1)S(1)} all-gather(bf16[128,1,2,96]{0,3,2,1:T(8,128)(2,1)S(1)} %fusion.23), channel_id=1, replica_groups=mesh['row'=8,'col'=8,'smp'=8] {'row'}, dimensions={0}, use_global_device_ids=true | all-gather | bytes 442368 | tf_op jit(solution)/shard_map/all_gather | solution.py:194
  242.2 0.5 fusion.151
  243.0 0.4 fusion.32
  243.4 1.8 fusion.15
  245.4 1.3 copy.45
  246.7 1.3 copy.46
  248.0 77.0 %all-reduce.7.cloned.1.call-done = bf16[1,128,768]{2,1,0:T(8,128)(2,1)} async-done(((bf16[1,128,768]{2,1,0:T(8,128)(2,1)}), bf16[1,128,768]{2,1,0:T(8,128)(2,1)}) %all-reduce.7.cloned.1.call-update) | async-done | bytes 196624 | tf_op jit(solution)/shard_map/psum | solution.py:207
  325.1 1.1 convert_reduce_fusion.2
  326.3 1.3 fusion.24
  327.6 1.3 convolution_bitcast_fusion.1
  328.9 21.5 %all_gather.22 = bf16[1024,1,2,96]{0,3,2,1:T(8,128)(2,1)S(1)} all-gather(bf16[128,1,2,96]{0,3,2,1:T(8,128)(2,1)S(1)} %fusion.24), channel_id=1, replica_groups=mesh['row'=8,'col'=8,'smp'=8] {'row'}, dimensions={0}, use_global_device_ids=true | all-gather | bytes 442368 | tf_op jit(solution)/shard_map/all_gather | solution.py:194
  350.5 0.5 fusion.152
  351.3 0.4 fusion.31
  351.7 0.9 fusion.16
  353.3 79.0 %all-reduce.9.cloned.1.call-done = bf16[1,128,768]{2,1,0:T(8,128)(2,1)} async-done(((bf16[1,128,768]{2,1,0:T(8,128)(2,1)}), bf16[1,128,768]{2,1,0:T(8,128)(2,1)}) %all-reduce.9.cloned.1.call-update) | async-done | bytes 196624 | tf_op jit(solution)/shard_map/psum | solution.py:207
  432.3 1.1 convert_reduce_fusion.1
  433.5 1.3 fusion.25
  434.8 1.3 convolution_bitcast_fusion
  436.1 21.4 %all_gather.23 = bf16[1024,1,2,96]{0,3,2,1:T(8,128)(2,1)S(1)} all-gather(bf16[128,1,2,96]{0,3,2,1:T(8,128)(2,1)S(1)} %fusion.25), channel_id=1, replica_groups=mesh['row'=8,'col'=8,'smp'=8] {'row'}, dimensions={0}, use_global_device_ids=true | all-gather | bytes 442368 | tf_op jit(solution)/shard_map/all_gather | solution.py:194
  457.6 0.5 fusion.153
  458.4 0.4 fusion.30
  458.8 0.9 fusion.17
  459.8 79.7 %all-reduce.11.cloned.1.call-done = bf16[1,128,768]{2,1,0:T(8,128)(2,1)} async-done(((bf16[1,128,768]{2,1,0:T(8,128)(2,1)}), bf16[1,128,768]{2,1,0:T(8,128)(2,1)}) %all-reduce.11.cloned.1.call-update) | async-done | bytes 196624 | tf_op jit(solution)/shard_map/psum | solution.py:207
  539.4 1.1 convert_reduce_fusion.5
  540.9 0.6 copy.49
  (102 shorter events, 6.3 us)
Async XLA Ops:
  7.2 4.8 copy-start
  14.3 17.0 %copy-start.8 = (f32[1,3]{1,0:T(1,128)S(1)}, f32[1,3]{1,0:T(1,128)}, u32[]{:S(2)}) copy-start(f32[1,3]{1,0:T(1,128)} %param.21) | copy-start | bytes 40
  14.3 17.6 %copy-start.14 = (s32[128]{0:T(128)S(1)}, s32[128]{0:T(128)}, u32[]{:S(2)}) copy-start(s32[128]{0:T(128)} %param.18) | copy-start | bytes 1540
  14.3 22.5 %copy-start.6 = (f32[3,8192]{1,0:T(4,128)S(1)}, f32[3,8192]{1,0:T(4,128)}, u32[]{:S(2)}) copy-start(f32[3,8192]{1,0:T(4,128)} %param.17) | copy-start | bytes 294916
  14.3 106.3 %all-to-all-start = ((bf16[4,128,128,1,16]{2,4,3,0,1:T(8,128)(2,1)}), bf16[4,128,128,1,16]{2,4,3,0,1:T(8,128)(2,1)S(1)}, u32[]{:S(2)}, u32[]{:S(2)}) async-start(bf16[4,128,128,1,16]{2,4,3,0,1:T(8,128)(2,1)} %bitcast.262), calls=%async_computation | async-start | bytes 4194304 | tf_op jit(solution)/shard_map/all_to_all | solution.py:74
  31.3 11.5 %copy-start.7 = (f32[4,768]{1,0:T(4,128)S(1)}, f32[4,768]{1,0:T(4,128)}, u32[]{:S(2)}) copy-start(f32[4,768]{1,0:T(4,128)} %param.24) | copy-start | bytes 36868
  31.3 185.6 %all-reduce.5.cloned.1.call-start = ((), (), s32[]{:S(2)}) async-start(), calls=%async_computation.1 | async-start | bytes 393216 | tf_op jit(solution)/shard_map/psum | solution.py:207
  36.8 6.2 %copy-start.11 = (f32[1,3,128]{2,0,1:T(1,128)S(1)}, f32[1,3,128]{2,0,1:T(1,128)}, u32[]{:S(2)}) copy-start(f32[1,3,128]{2,0,1:T(1,128)} %param.23) | copy-start | bytes 4612
  36.9 6.3 %copy-start.5 = (bf16[128,768]{1,0:T(8,128)(2,1)S(1)}, bf16[128,768]{1,0:T(8,128)(2,1)}, u32[]{:S(2)}) copy-start(bf16[128,768]{1,0:T(8,128)(2,1)} %param.15) | copy-start | bytes 589828
  36.9 8.1 %copy-start.9 = (s32[128]{0:T(128)S(1)}, s32[128]{0:T(128)}, u32[]{:S(2)}) copy-start(s32[128]{0:T(128)} %param.19) | copy-start | bytes 1540
  36.9 49.2 %copy-start.12 = (s32[128]{0:T(128)S(1)}, s32[128]{0:T(128)}, u32[]{:S(2)}) copy-start(s32[128]{0:T(128)} %param.20) | copy-start | bytes 1540
  36.9 60.7 %copy-start.10 = (f32[4,16]{1,0:T(4,128)S(1)}, f32[4,16]{1,0:T(4,128)}, u32[]{:S(2)}) copy-start(f32[4,16]{1,0:T(4,128)} %param.26) | copy-start | bytes 772
  128.5 196.6 %all-reduce.7.cloned.1.call-start = ((), (), s32[]{:S(2)}) async-start(), calls=%async_computation.2 | async-start | bytes 393216 | tf_op jit(solution)/shard_map/psum | solution.py:207
  131.2 111.0 %copy-start.1 = (f32[2,128,1024]{2,1,0:T(8,128)S(1)}, f32[2,128,1024]{2,1,0:T(8,128)}, u32[]{:S(2)}) copy-start(f32[2,128,1024]{2,1,0:T(8,128)} %copy.44) | copy-start | bytes 3145732
  245.3 187.0 %all-reduce.9.cloned.1.call-start = ((), (), s32[]{:S(2)}) async-start(), calls=%async_computation.3 | async-start | bytes 393216 | tf_op jit(solution)/shard_map/psum | solution.py:207
  248.0 102.4 %copy-start.2 = (f32[2,128,1024]{2,1,0:T(8,128)S(1)}, f32[2,128,1024]{2,1,0:T(8,128)}, u32[]{:S(2)}) copy-start(f32[2,128,1024]{2,1,0:T(8,128)} %copy.46) | copy-start | bytes 3145732
  350.4 1.2 copy-start.4
  352.6 186.8 %all-reduce.11.cloned.1.call-start = ((), (), s32[]{:S(2)}) async-start(), calls=%async_computation.4 | async-start | bytes 393216 | tf_op jit(solution)/shard_map/psum | solution.py:207
  458.1 82.6 %copy-start.13 = (bf16[3,768]{1,0:T(4,128)(2,1)S(1)}, bf16[3,768]{1,0:T(4,128)(2,1)}, u32[]{:S(2)}) copy-start(bf16[3,768]{1,0:T(4,128)(2,1)} %param.29) | copy-start | bytes 13828
  540.5 1.1 copy-start.3
Sparse Core Ops, SparseCore 0:
  128.6 88.2 all-reduce.4
  245.4 79.6 all-reduce.6
  352.7 79.4 all-reduce.8
  459.8 79.5 all-reduce.10
where the time goes:
time: 549 us; the launch traced here: 548 us
  waiting for transfers between devices  321 us (58%)
  blocking collectives  138 us (25%)
  matrix products  20.9 us (4%)
  between operations  19.3 us (4%)
  starting transfers between devices  17.3 us (3%)
  local copies, waits for them, and re-layouts  16.9 us (3%)
  other arithmetic  14 us (3%)
    psum x4, waiting for transfers between devices, body(): lax.psum(partial_out.astype(jnp.bfloat16), 'col').astype(jnp.float32)  321 us
    all_gather x4, blocking collectives, body(): lax.all_gather(key_value, 'row', axis=0, tiled=True)  85.7 us
    all_gather x1, blocking collectives, body(): lax.all_gather(chain_label, 'row', axis=0, tiled=True)  41.1 us
    all_to_all x1, starting transfers between devices, relay_bias(): lax.all_to_all(spread, ('col', 'smp'), split_axis=1, concat_axis=3, tiled...  16.9 us
    all_gather x1, blocking collectives, body(): lax.all_gather(padding_key_mask, 'row', axis=0, tiled=True)  11.5 us
  transfers between devices with their start and end apart: 5, of which 4 were waited for; matrix products, arithmetic and copies ran while one was open for 3% of the time, Pallas kernels for 0%

commit v1 on v0

--- a/solution.py
+++ b/solution.py
@@ -204,7 +204,9 @@
             attention_output_weight[block_index],
             preferred_element_type=jnp.float32,
         )
-        summed = lax.psum(partial_out.astype(jnp.bfloat16), "col").astype(jnp.float32)
+        summed = jnp.sum(lax.all_gather(partial_out.astype(jnp.bfloat16), "col"), axis=0).astype(
+            jnp.float32
+        )
         hidden_activity = (hidden_activity.astype(jnp.float32) + summed).astype(jnp.bfloat16)
     final_normed = layer_norm(hidden_activity.astype(jnp.float32)).astype(jnp.bfloat16)
     update = jnp.einsum(

time: 549 us -> 385 us (0.70)
  the two profiles are of different devices: /device:TPU:17 before, /device:TPU:1 now
where the time goes in v1:
time: 385 us; the launch traced here: 384 us
  waiting for transfers between devices  153 us (40%)
  blocking collectives  139 us (36%)
  matrix products  21 us (5%)
  between operations  19.3 us (5%)
  starting transfers between devices  17.9 us (5%)
  other arithmetic  17 us (4%)
  local copies, waits for them, and re-layouts  16.8 us (4%)
    all_gather x4, waiting for transfers between devices, body(): lax.all_gather(partial_out.astype(jnp.bfloat16), 'col')  153 us
    all_gather x4, blocking collectives, body(): lax.all_gather(key_value, 'row', axis=0, tiled=True)  85.9 us
    all_gather x1, blocking collectives, body(): lax.all_gather(chain_label, 'row', axis=0, tiled=True)  41.7 us
    all_to_all x1, starting transfers between devices, relay_bias(): lax.all_to_all(spread, ('col', 'smp'), split_axis=1, concat_axis=3, tiled...  17.8 us
    all_gather x1, blocking collectives, body(): lax.all_gather(padding_key_mask, 'row', axis=0, tiled=True)  11.5 us
  transfers between devices with their start and end apart: 5, of which 4 were waited for; matrix products, arithmetic and copies ran while one was open for 4% of the time, Pallas kernels for 0%

profile of v1, /device:TPU:1, one launch (start us, length us, event | category | flops | bytes accessed | tf_op | source)
XLA Modules:
  0.0 384.2 jit_solution(1937159168932150434)
XLA Ops:
  7.2 1.4 convert_reduce_fusion
  8.6 1.7 fusion.32
  10.3 1.6 fusion.46
  12.4 1.9 broadcast_in_dim.47
  14.3 17.8 %all-to-all-start = ((bf16[4,128,128,1,16]{2,4,3,0,1:T(8,128)(2,1)}), bf16[4,128,128,1,16]{2,4,3,0,1:T(8,128)(2,1)S(1)}, u32[]{:S(2)}, u32[]{:S(2)}) async-start(bf16[4,128,128,1,16]{2,4,3,0,1:T(8,128)(2,1)} %bitcast.246), calls=%async_computation | async-start | bytes 4194304 | tf_op jit(solution)/shard_map/all_to_all | solution.py:74
  32.2 0.6 fusion.143
  37.7 2.6 copy.35
  40.4 2.8 gather_fusion
  44.5 1.3 convolution_bitcast_fusion.3
  45.8 41.7 %all-gather.5 = s32[8,1,128]{2,1,0:T(1,128)S(1)} all-gather(s32[1,1,128]{2,1,0:T(1,128)S(1)} %bitcast.279), channel_id=1, replica_groups=mesh['row'=8,'col'=8,'smp'=8] {'row'}, dimensions={0}, use_global_device_ids=true | all-gather | bytes 4608 | tf_op jit(solution)/shard_map/all_gather | solution.py:151
  87.6 11.5 %all-gather.4 = s32[8,1,128]{2,1,0:T(1,128)S(1)} all-gather(s32[1,1,128]{2,1,0:T(1,128)S(1)} %bitcast.280), channel_id=1, replica_groups=mesh['row'=8,'col'=8,'smp'=8] {'row'}, dimensions={0}, use_global_device_ids=true | all-gather | bytes 4608 | tf_op jit(solution)/shard_map/all_gather | solution.py:152
  99.1 1.3 fusion.18
  100.4 21.4 %all_gather.43 = bf16[1024,1,2,96]{0,3,2,1:T(8,128)(2,1)S(1)} all-gather(bf16[128,1,2,96]{0,3,2,1:T(8,128)(2,1)S(1)} %fusion.18), channel_id=1, replica_groups=mesh['row'=8,'col'=8,'smp'=8] {'row'}, dimensions={0}, use_global_device_ids=true | all-gather | bytes 442368 | tf_op jit(solution)/shard_map/all_gather | solution.py:194
  122.3 1.8 slice_convert_fusion
  124.2 1.3 copy.42
  125.5 1.7 fusion.144
  127.6 0.4 fusion.29
  128.0 1.8 convolution_convert_fusion.4
  129.9 1.3 copy.43
  131.2 1.3 copy.44
  132.5 42.8 %all-gather.11.cloned.1.call-done = bf16[1024,768]{1,0:T(8,128)(2,1)} async-done(((bf16[128,768]{1,0:T(8,128)(2,1)}), bf16[1024,768]{1,0:T(8,128)(2,1)}) %all-gather.11.cloned.1.call-update) | async-done | bytes 1572880 | tf_op jit(solution)/shard_map/all_gather | solution.py:207
  175.3 1.7 reduce.44
  177.4 1.3 fusion.19
  178.7 1.3 convolution_bitcast_fusion.2
  180.0 21.4 %all_gather.47 = bf16[1024,1,2,96]{0,3,2,1:T(8,128)(2,1)S(1)} all-gather(bf16[128,1,2,96]{0,3,2,1:T(8,128)(2,1)S(1)} %fusion.19), channel_id=1, replica_groups=mesh['row'=8,'col'=8,'smp'=8] {'row'}, dimensions={0}, use_global_device_ids=true | all-gather | bytes 442368 | tf_op jit(solution)/shard_map/all_gather | solution.py:194
  201.5 0.5 fusion.145
  202.7 1.8 convolution_convert_fusion.3
  204.7 1.3 copy.45
  206.0 1.3 copy.46
  207.3 35.1 %all-gather.13.cloned.1.call-done = bf16[1024,768]{1,0:T(8,128)(2,1)} async-done(((bf16[128,768]{1,0:T(8,128)(2,1)}), bf16[1024,768]{1,0:T(8,128)(2,1)}) %all-gather.13.cloned.1.call-update) | async-done | bytes 1572880 | tf_op jit(solution)/shard_map/all_gather | solution.py:207
  242.4 1.7 reduce.45
  244.5 1.3 fusion.20
  245.8 1.3 convolution_bitcast_fusion.1
  247.1 21.6 %all_gather.50 = bf16[1024,1,2,96]{0,3,2,1:T(8,128)(2,1)S(1)} all-gather(bf16[128,1,2,96]{0,3,2,1:T(8,128)(2,1)S(1)} %fusion.20), channel_id=1, replica_groups=mesh['row'=8,'col'=8,'smp'=8] {'row'}, dimensions={0}, use_global_device_ids=true | all-gather | bytes 442368 | tf_op jit(solution)/shard_map/all_gather | solution.py:194
  268.8 0.5 fusion.146
  269.6 0.4 fusion.27
  270.0 0.9 convolution_convert_fusion.2
  271.4 37.4 %all-gather.15.cloned.1.call-done = bf16[1024,768]{1,0:T(8,128)(2,1)} async-done(((bf16[128,768]{1,0:T(8,128)(2,1)}), bf16[1024,768]{1,0:T(8,128)(2,1)}) %all-gather.15.cloned.1.call-update) | async-done | bytes 1572880 | tf_op jit(solution)/shard_map/all_gather | solution.py:207
  308.8 1.6 reduce.46
  310.8 1.3 fusion.21
  312.1 1.3 convolution_bitcast_fusion
  313.4 21.5 %all_gather.53 = bf16[1024,1,2,96]{0,3,2,1:T(8,128)(2,1)S(1)} all-gather(bf16[128,1,2,96]{0,3,2,1:T(8,128)(2,1)S(1)} %fusion.21), channel_id=1, replica_groups=mesh['row'=8,'col'=8,'smp'=8] {'row'}, dimensions={0}, use_global_device_ids=true | all-gather | bytes 442368 | tf_op jit(solution)/shard_map/all_gather | solution.py:194
  334.9 0.5 fusion.147
  335.7 0.4 fusion.26
  336.1 0.9 convolution_convert_fusion.1
  337.1 37.8 %all-gather.17.cloned.1.call-done = bf16[1024,768]{1,0:T(8,128)(2,1)} async-done(((bf16[128,768]{1,0:T(8,128)(2,1)}), bf16[1024,768]{1,0:T(8,128)(2,1)}) %all-gather.17.cloned.1.call-update) | async-done | bytes 1572880 | tf_op jit(solution)/shard_map/all_gather | solution.py:207
  374.9 1.6 reduce.47
  377.1 0.6 copy.49
  (106 shorter events, 6.7 us)
Async XLA Ops:
  7.2 4.8 %copy-start = (bf16[128,4,16]{0,2,1:T(8,128)(2,1)S(1)}, bf16[128,4,16]{0,2,1:T(8,128)(2,1)}, u32[]{:S(2)}) copy-start(bf16[128,4,16]{0,2,1:T(8,128)(2,1)} %param.25) | copy-start | bytes 49156
  14.3 17.8 %copy-start.8 = (f32[1,3]{1,0:T(1,128)S(1)}, f32[1,3]{1,0:T(1,128)}, u32[]{:S(2)}) copy-start(f32[1,3]{1,0:T(1,128)} %param.21) | copy-start | bytes 40
  14.3 18.4 %copy-start.14 = (s32[128]{0:T(128)S(1)}, s32[128]{0:T(128)}, u32[]{:S(2)}) copy-start(s32[128]{0:T(128)} %param.18) | copy-start | bytes 1540
  14.3 23.4 %copy-start.6 = (f32[3,8192]{1,0:T(4,128)S(1)}, f32[3,8192]{1,0:T(4,128)}, u32[]{:S(2)}) copy-start(f32[3,8192]{1,0:T(4,128)} %param.17) | copy-start | bytes 294916
  14.3 107.6 %all-to-all-start = ((bf16[4,128,128,1,16]{2,4,3,0,1:T(8,128)(2,1)}), bf16[4,128,128,1,16]{2,4,3,0,1:T(8,128)(2,1)S(1)}, u32[]{:S(2)}, u32[]{:S(2)}) async-start(bf16[4,128,128,1,16]{2,4,3,0,1:T(8,128)(2,1)} %bitcast.246), calls=%async_computation | async-start | bytes 4194304 | tf_op jit(solution)/shard_map/all_to_all | solution.py:74
  32.1 11.5 %copy-start.7 = (f32[4,768]{1,0:T(4,128)S(1)}, f32[4,768]{1,0:T(4,128)}, u32[]{:S(2)}) copy-start(f32[4,768]{1,0:T(4,128)} %param.24) | copy-start | bytes 36868
  32.1 143.2 %all-gather.11.cloned.1.call-start = ((), (), s32[]{:S(2)}) async-start(), calls=%async_computation.1 | async-start | bytes 1769472 | tf_op jit(solution)/shard_map/all_gather | solution.py:207
  37.7 6.2 %copy-start.11 = (f32[1,3,128]{2,0,1:T(1,128)S(1)}, f32[1,3,128]{2,0,1:T(1,128)}, u32[]{:S(2)}) copy-start(f32[1,3,128]{2,0,1:T(1,128)} %param.23) | copy-start | bytes 4612
  37.7 6.3 %copy-start.5 = (bf16[128,768]{1,0:T(8,128)(2,1)S(1)}, bf16[128,768]{1,0:T(8,128)(2,1)}, u32[]{:S(2)}) copy-start(bf16[128,768]{1,0:T(8,128)(2,1)} %param.15) | copy-start | bytes 589828
  37.7 8.1 %copy-start.9 = (s32[128]{0:T(128)S(1)}, s32[128]{0:T(128)}, u32[]{:S(2)}) copy-start(s32[128]{0:T(128)} %param.19) | copy-start | bytes 1540
  37.7 49.8 %copy-start.12 = (s32[128]{0:T(128)S(1)}, s32[128]{0:T(128)}, u32[]{:S(2)}) copy-start(s32[128]{0:T(128)} %param.20) | copy-start | bytes 1540
  37.7 61.3 %copy-start.10 = (f32[4,16]{1,0:T(4,128)S(1)}, f32[4,16]{1,0:T(4,128)}, u32[]{:S(2)}) copy-start(f32[4,16]{1,0:T(4,128)} %param.26) | copy-start | bytes 772
  129.8 112.6 %all-gather.13.cloned.1.call-start = ((), (), s32[]{:S(2)}) async-start(), calls=%async_computation.2 | async-start | bytes 1769472 | tf_op jit(solution)/shard_map/all_gather | solution.py:207
  175.3 26.2 %copy-start.1 = (f32[2,128,1024]{2,1,0:T(8,128)S(1)}, f32[2,128,1024]{2,1,0:T(8,128)}, u32[]{:S(2)}) copy-start(f32[2,128,1024]{2,1,0:T(8,128)} %copy.44) | copy-start | bytes 3145732
  204.6 104.2 %all-gather.15.cloned.1.call-start = ((), (), s32[]{:S(2)}) async-start(), calls=%async_computation.3 | async-start | bytes 1769472 | tf_op jit(solution)/shard_map/all_gather | solution.py:207
  242.4 26.4 %copy-start.2 = (f32[2,128,1024]{2,1,0:T(8,128)S(1)}, f32[2,128,1024]{2,1,0:T(8,128)}, u32[]{:S(2)}) copy-start(f32[2,128,1024]{2,1,0:T(8,128)} %copy.46) | copy-start | bytes 3145732
  268.8 1.2 copy-start.4
  271.0 103.9 %all-gather.17.cloned.1.call-start = ((), (), s32[]{:S(2)}) async-start(), calls=%async_computation.4 | async-start | bytes 1769472 | tf_op jit(solution)/shard_map/all_gather | solution.py:207
  335.7 41.2 %copy-start.13 = (bf16[3,768]{1,0:T(4,128)(2,1)S(1)}, bf16[3,768]{1,0:T(4,128)(2,1)}, u32[]{:S(2)}) copy-start(bf16[3,768]{1,0:T(4,128)(2,1)} %param.29) | copy-start | bytes 13828
  376.6 1.1 copy-start.3
Sparse Core Ops, SparseCore 0:
  129.9 45.3 all-gather.10
  204.7 37.6 all-gather.12
  271.1 37.6 all-gather.14
  337.2 37.6 all-gather.16
